TPU v7x, 32 devices: a whole 2x2x4 slice. The times are simulated.
32 devices in a mesh: cp: 2 (over y), tp: 4 (over x, core), ep: 4 (over z).
Axes of the slice: x: 2, y: 2, z: 4, core: 2. Of those that a mesh axis runs over, the one named last changes fastest.
Arguments:
- query: bfloat16 [8, 512, 4096], P('ep', 'cp', 'tp'), may hold values from -6 to 6
- keys: bfloat16 [8, 512, 512], P('ep', 'cp', 'tp'), may hold values from -6 to 6
- values: bfloat16 [8, 512, 512], P('ep', 'cp', 'tp'), may hold values from -24 to 24
- segment_ids: int32 [8, 512], P('ep', 'cp'), may hold values from 0 to 3, never falling along the last dimension, each value on 1 to 256 neighbouring positions
- query_norm_gain: float32 [128], replicated, may hold values from 0.25 to 1.75
- key_norm_gain: float32 [128], replicated, may hold values from 0.25 to 1.75
- out_weight: bfloat16 [4096, 2048], P('tp', 'cp'), may hold values from -0.09375 to 0.09375
- residual: bfloat16 [8, 512, 2048], P('ep', 'cp'), may hold values from -3 to 3
- norm_gain: float32 [2048], replicated, may hold values from 0.25 to 1.75
- router_weight: bfloat16 [2048, 16], replicated, may hold values from -0.125 to 0.125
- expert_ids: int32 [8, 512, 8], P('ep', 'cp'), may hold values from 0 to 15, all different within a row; in each aligned block of 64 rows (0 to 63, 64 to 127, ..., all dimensions but the last counted through in order) at most 36 rows name the same one
- expert_gate: bfloat16 [16, 2048, 768], P(('tp', 'ep'), None, 'cp'), may hold values from -0.125 to 0.125
- expert_up: bfloat16 [16, 2048, 768], P(('tp', 'ep'), None, 'cp'), may hold values from -0.125 to 0.125
- expert_down: bfloat16 [16, 2048, 768], P(('tp', 'ep'), None, 'cp'), may hold values from -0.21875 to 0.21875
Outputs:
- layer_out: bfloat16 [8, 512, 2048], P('ep', ('cp', 'tp'))
Inputs may be any that keep to these rules, and one draw needn't show every extreme that they name: `segment_ids`: document numbers never fall along a sequence. `expert_ids`: each token names 8 different experts; in every aligned block of 64 positions of a sequence no expert is named by more than 36 tokens, a bound that some block reaches.
All inputs are finite; a program needn't handle non-finite values.
Results may differ from a plain program's by a relative error of at most 0.007.
Values may be sent and summed in bfloat16 or wider, within the bound.
No kernel may reach another device: no remote copies, remote signals or barrier semaphores. Data moves between devices by JAX's collectives and lax.ppermute only.
A program may use at most 128 MiB of HBM per device.

v0:
```python
import jax
import jax.numpy as jnp
from jax import lax
from jax.sharding import PartitionSpec as P

HEAD_WIDTH = 128


def root_mean_scale(entries, gain):
    mean_sq = jnp.mean(entries * entries, axis=-1, keepdims=True)
    return entries * lax.rsqrt(mean_sq + 1e-06) * gain


def capacity(share, top_count, experts):
    return min(
        share, max(2, share * top_count // experts + max(1, share * top_count // (8 * experts)))
    )


def slot_numbers(ids, experts):
    flat_ids = ids.reshape(-1)
    table = (flat_ids[:, None] == jnp.arange(experts, dtype=jnp.int32)[None, :]).astype(jnp.int32)
    before = jnp.cumsum(table, axis=0) - table
    return jnp.sum(before * table, axis=1).reshape(ids.shape)


def route(state, ids, norm_gain, router_weight):
    normed = root_mean_scale(state, norm_gain).astype(jnp.bfloat16)
    logits = jnp.dot(normed, router_weight, preferred_element_type=jnp.float32)
    experts = router_weight.shape[1]
    picks = ids[:, :, None] == jnp.arange(experts, dtype=jnp.int32)[None, None, :]
    chosen = jnp.sum(jnp.where(picks, logits[:, None, :], jnp.float32(0.0)), axis=-1)
    raised = jnp.exp(chosen)
    return (normed, raised / jnp.sum(raised, axis=-1, keepdims=True))


def expert_rows(received, full_gate, full_up, full_down):
    width = received.shape[-1]
    flat_rows = received.reshape(-1, width)
    gate_act = jnp.dot(flat_rows, full_gate[0], preferred_element_type=jnp.float32)
    up_act = jnp.dot(flat_rows, full_up[0], preferred_element_type=jnp.float32)
    hidden_act = (jax.nn.silu(gate_act) * up_act).astype(jnp.bfloat16)
    served = jnp.einsum(
        "rf,df->rd", hidden_act, full_down[0], preferred_element_type=jnp.float32
    ).astype(jnp.bfloat16)
    return served.reshape(received.shape)


def shards(
    query,
    keys,
    values,
    segment_ids,
    query_norm_gain,
    key_norm_gain,
    out_weight,
    residual,
    norm_gain,
    router_weight,
    expert_ids,
    expert_gate,
    expert_up,
    expert_down,
):
    packs = query.shape[0]
    row_count = query.shape[1]
    head_count = query.shape[2] // HEAD_WIDTH
    width = residual.shape[2]
    experts = router_weight.shape[1]
    top_count = expert_ids.shape[2]
    score_scale = HEAD_WIDTH ** (-0.5)
    query_rows_normed = root_mean_scale(
        query.astype(jnp.float32).reshape(packs, row_count, head_count, HEAD_WIDTH), query_norm_gain
    ).astype(jnp.bfloat16)
    key_rows_normed = root_mean_scale(keys.astype(jnp.float32), key_norm_gain).astype(jnp.bfloat16)
    own_docs = segment_ids.astype(jnp.bfloat16)
    key_piece = lax.all_gather(key_rows_normed, "cp", axis=1, tiled=True)
    value_piece = lax.all_gather(values, "cp", axis=1, tiled=True)
    doc_piece = lax.all_gather(own_docs, "cp", axis=1, tiled=True)
    scores = (
        jnp.einsum(
            "pshd,pnd->phsn", query_rows_normed, key_piece, preferred_element_type=jnp.float32
        )
        * score_scale
    )
    same_doc = own_docs[:, :, None] == doc_piece[:, None, :]
    probs = jnp.where(same_doc[:, None], jnp.exp(scores), jnp.float32(0.0))
    denom = jnp.sum(probs, axis=-1)
    probs_b = probs.astype(jnp.bfloat16)
    summed = jnp.einsum("phsn,pnd->pshd", probs_b, value_piece, preferred_element_type=jnp.float32)
    denom, summed = (denom, summed)
    attn = (
        (summed / jnp.transpose(denom, (0, 2, 1))[:, :, :, None])
        .astype(jnp.bfloat16)
        .reshape(packs * row_count, head_count * HEAD_WIDTH)
    )
    partial_proj = jnp.dot(
        attn,
        lax.all_gather(out_weight, "cp", axis=1, tiled=True),
        preferred_element_type=jnp.float32,
    ).reshape(packs, row_count, width)
    full_gate, full_up, full_down = (
        lax.all_gather(expert_gate, "cp", axis=2, tiled=True),
        lax.all_gather(expert_up, "cp", axis=2, tiled=True),
        lax.all_gather(expert_down, "cp", axis=2, tiled=True),
    )
    share = row_count // lax.axis_size("tp")
    tp_index = lax.axis_index("tp")
    cap = capacity(share, top_count, experts)
    projected = lax.psum_scatter(partial_proj, "tp", scatter_dimension=1, tiled=True)
    first_row = tp_index * share
    state = lax.dynamic_slice_in_dim(residual, first_row, share, 1).astype(jnp.float32) + projected
    local_ids = lax.dynamic_slice_in_dim(expert_ids, first_row, share, 1).reshape(
        packs * share, top_count
    )
    normed, gates = route(state.reshape(packs * share, width), local_ids, norm_gain, router_weight)
    dev_cap = packs * cap
    slots = slot_numbers(local_ids, experts)
    target = (local_ids * dev_cap + slots).reshape(-1)
    sent_rows = jnp.broadcast_to(normed[:, None, :], (packs * share, top_count, width)).reshape(
        -1, width
    )
    buffer = (
        jnp.zeros((experts * dev_cap, width), jnp.bfloat16)
        .at[target]
        .set(sent_rows)
        .reshape(experts, dev_cap, width)
    )
    served = expert_rows(
        lax.all_to_all(buffer, ("tp", "ep"), split_axis=0, concat_axis=0, tiled=True),
        full_gate,
        full_up,
        full_down,
    )
    back = lax.all_to_all(served, ("tp", "ep"), split_axis=0, concat_axis=0, tiled=True)
    picked = back.reshape(experts * dev_cap, width)[target].reshape(packs * share, top_count, width)
    mixture = jnp.sum(gates[:, :, None] * picked.astype(jnp.float32), axis=1)
    layer_out = (state + mixture.reshape(packs, share, width)).astype(jnp.bfloat16)
    return layer_out


def solution(mesh):
    return jax.shard_map(
        shards,
        mesh=mesh,
        in_specs=(
            P("ep", "cp", "tp"),
            P("ep", "cp", "tp"),
            P("ep", "cp", "tp"),
            P("ep", "cp"),
            P(),
            P(),
            P("tp", "cp"),
            P("ep", "cp", None),
            P(),
            P(),
            P("ep", "cp", None),
            P(("tp", "ep"), None, "cp"),
            P(("tp", "ep"), None, "cp"),
            P(("tp", "ep"), None, "cp"),
        ),
        out_specs=P("ep", ("cp", "tp"), None),
        check_vma=False,
    )
```

profile of v0, /device:TPU:0, one launch (start us, length us, event | category | flops | bytes accessed | tf_op | source)
XLA Modules:
  0.0 424.7 jit_solution(739500518917911366)
XLA Ops:
  8.0 1.5 copy.74
  10.5 5.2 %all_gather.21 = bf16[2,512]{1,0:T(2,128)(2,1)S(1)} all-gather(bf16[2,256]{1,0:T(2,128)(2,1)S(1)} %convert_element_type.52), channel_id=1, replica_groups=mesh['cp'=2,'tp'=4,'ep'=4] {'cp'}, dimensions={1}, use_global_device_ids=true | all-gather | bytes 3072 | tf_op jit(solution)/shard_map/all_gather | solution.py:79
  16.0 5.7 %all_gather.22 = bf16[2,512,128]{2,1,0:T(8,128)(2,1)S(1)} all-gather(bf16[2,256,128]{2,1,0:T(8,128)(2,1)S(1)} %fusion.31), channel_id=1, replica_groups=mesh['cp'=2,'tp'=4,'ep'=4] {'cp'}, dimensions={1}, use_global_device_ids=true | all-gather | bytes 393216 | tf_op jit(solution)/shard_map/all_gather | solution.py:77
  21.6 8.7 %all_gather.23 = bf16[2,512,128]{1,2,0:T(8,128)(2,1)S(1)} all-gather(bf16[2,256,128]{1,2,0:T(8,128)(2,1)S(1)} %copy.60), channel_id=1, replica_groups=mesh['cp'=2,'tp'=4,'ep'=4] {'cp'}, dimensions={1}, use_global_device_ids=true | all-gather | bytes 393216 | tf_op jit(solution)/shard_map/all_gather | solution.py:78
  31.3 2.2 fusion.1
  33.5 1.7 fusion.21
  35.2 35.5 %all-gather.5.cloned.1.call-done = bf16[1024,2048]{1,0:T(8,128)(2,1)} async-done(((bf16[1024,1024]{1,0:T(8,128)(2,1)}), bf16[1024,2048]{1,0:T(8,128)(2,1)}) %all-gather.5.cloned.1.call-update) | async-done | bytes 4194320 | tf_op jit(solution)/shard_map/all_gather | solution.py:99
  70.7 6.5 %fusion.7 = f32[2,256,2048]{2,1,0:T(8,128)} fusion(bf16[2,256,1024]{1,2,0:T(8,128)(2,1)S(1)} %bitcast.104, bf16[1024,2048]{1,0:T(8,128)(2,1)} %all-gather.5.cloned.1.call-done), kind=kOutput, calls=%fused_computation.11 | convolution fusion | flops 2147483648 | bytes 9437184 | tf_op jit(solution)/shard_map/dot_general | solution.py:97
  78.3 4.5 %reduce-window.6 = s32[16,8,128]{2,1,0:T(8,128)S(1)} reduce-window(s32[16,8,128]{2,1,0:T(8,128)S(1)} %fusion.37, s32[]{:T(128)} %constant.14.clone.1), window={size=1x1x128 pad=0_0x0_0x127_0}, to_apply=%region_7.8 | reduce-window | flops 2080768 | bytes 131076 | tf_op jit(solution)/shard_map/reduce-window
  83.5 39.1 %reduce-scatter.2.cloned.1.call-done = f32[2,64,2048]{2,1,0:T(8,128)} async-done(((f32[2,256,2048]{2,1,0:T(8,128)}), f32[2,64,2048]{2,1,0:T(8,128)}) %reduce-scatter.2.cloned.1.call-update) | async-done | bytes 1048592 | tf_op jit(solution)/shard_map/reduce_scatter | solution.py:110
  122.6 1.6 multiply_reduce_fusion
  124.5 9.4 %scatter_custom_fusion = bf16[1152,2048]{1,0:T(8,128)(2,1)} fusion(s32[1024]{0:T(1024)S(1)} %bitcast.109, bf16[]{:T(256)} %constant.37.clone.1, bf16[128,2048]{1,0:T(8,128)(2,1)S(1)} %fusion.26), kind=kCustom, calls=%fused_computation.9 | custom fusion | bytes 5242882 | tf_op jit(solution)/shard_map/scatter | solution.py:126
  133.8 4.8 %all-to-all-start = ((bf16[16,72,2048]{2,1,0:T(8,128)(2,1)}), bf16[16,72,2048]{2,1,0:T(8,128)(2,1)}, u32[]{:S(2)}, u32[]{:S(2)}) async-start(bf16[16,72,2048]{2,1,0:T(8,128)(2,1)} %bitcast.101), calls=%async_computation.1 | async-start | bytes 9437184 | tf_op jit(solution)/shard_map/all_to_all | solution.py:130
  140.5 46.8 %all-gather.7.cloned.1.call-done = bf16[1,2048,768]{2,1,0:T(8,128)(2,1)} async-done(((bf16[1,2048,384]{2,1,0:T(8,128)(2,1)}), bf16[1,2048,768]{2,1,0:T(8,128)(2,1)}) %all-gather.7.cloned.1.call-update) | async-done | bytes 3145744 | tf_op jit(solution)/shard_map/all_gather | solution.py:103
  187.3 57.0 %all-to-all-done = bf16[16,72,2048]{2,1,0:T(8,128)(2,1)} async-done(((bf16[16,72,2048]{2,1,0:T(8,128)(2,1)}), bf16[16,72,2048]{2,1,0:T(8,128)(2,1)}, u32[]{:S(2)}, u32[]{:S(2)}) %all-to-all-start) | async-done | bytes 4718624 | tf_op jit(solution)/shard_map/all_to_all | solution.py:130
  244.3 9.4 %fusion.15 = f32[1152,768]{1,0:T(8,128)} fusion(bf16[1152,2048]{1,0:T(8,128)(2,1)} %bitcast.16, bf16[1,2048,768]{2,1,0:T(8,128)(2,1)} %all-gather.7.cloned.1.call-done), kind=kOutput, calls=%fused_computation.20 | convolution fusion | flops 3623878656 | bytes 11403264 | tf_op jit(solution)/shard_map/dot_general | solution.py:40
  253.7 8.5 %fusion.12 = bf16[1152,768]{1,0:T(8,128)(2,1)S(1)} fusion(bf16[1152,2048]{1,0:T(8,128)(2,1)} %bitcast.16, f32[1152,768]{1,0:T(8,128)} %fusion.15, bf16[1,2048,768]{2,1,0:T(8,128)(2,1)} %all-gather.9.cloned.1.call-done), kind=kOutput, calls=%fused_computation.17 | convolution fusion | flops 3629187072 | bytes 13172736 | tf_op jit(solution)/shard_map/dot_general | solution.py:41
  262.2 18.0 %all-gather.11.cloned.1.call-done = bf16[1,2048,768]{2,1,0:T(8,128)(2,1)} async-done(((bf16[1,2048,384]{2,1,0:T(8,128)(2,1)}), bf16[1,2048,768]{2,1,0:T(8,128)(2,1)}) %all-gather.11.cloned.1.call-update) | async-done | bytes 3145744 | tf_op jit(solution)/shard_map/all_gather | solution.py:105
  280.1 7.4 %convolution_convert_fusion = bf16[1152,2048]{1,0:T(8,128)(2,1)} fusion(bf16[1152,768]{1,0:T(8,128)(2,1)S(1)} %fusion.12, bf16[1,2048,768]{2,1,0:T(8,128)(2,1)} %all-gather.11.cloned.1.call-done), kind=kOutput, calls=%fused_computation.5 | convolution fusion | flops 3626237952 | bytes 9633792 | tf_op jit(solution)/shard_map/rf,df->rd/dot_general | solution.py:43
  287.6 5.7 %all-to-all-start.1 = ((bf16[16,72,2048]{2,1,0:T(8,128)(2,1)}), bf16[16,72,2048]{2,1,0:T(8,128)(2,1)}, u32[]{:S(2)}, u32[]{:S(2)}) async-start(bf16[16,72,2048]{2,1,0:T(8,128)(2,1)} %bitcast.102), calls=%async_computation.2 | async-start | bytes 9437184 | tf_op jit(solution)/shard_map/all_to_all | solution.py:135
  293.8 105.2 %all-to-all-done.1 = bf16[16,72,2048]{2,1,0:T(8,128)(2,1)} async-done(((bf16[16,72,2048]{2,1,0:T(8,128)(2,1)}), bf16[16,72,2048]{2,1,0:T(8,128)(2,1)}, u32[]{:S(2)}, u32[]{:S(2)}) %all-to-all-start.1) | async-done | bytes 4718624 | tf_op jit(solution)/shard_map/all_to_all | solution.py:135
  398.9 11.8 %gather_fusion = bf16[1024,2048]{1,0:T(8,128)(2,1)} fusion(bf16[1152,2048]{1,0:T(8,128)(2,1)} %bitcast.21, s32[1024]{0:T(1024)S(1)} %broadcast_clamp_fusion), kind=kCustom, calls=%fused_computation | custom fusion | bytes 8392704 | tf_op jit(solution)/shard_map/gather | solution.py:136
  410.7 6.5 %fusion = f32[128,2048]{1,0:T(8,128)S(1)} fusion(bf16[1024,2048]{1,0:T(8,128)(2,1)} %gather_fusion, f32[128,8]{1,0:T(8,128)S(1)} %copy.64), kind=kLoop, calls=%fused_computation.3 | loop fusion | flops 6029312 | bytes 5246976 | tf_op jit(solution)/shard_map/reduce_sum | solution.py:137
  417.3 0.9 add_convert_fusion
  (62 shorter events, 8.0 us)
Async XLA Ops:
  6.5 286.8 %copy-start = (bf16[2048,16]{0,1:T(8,128)(2,1)S(1)}, bf16[2048,16]{0,1:T(8,128)(2,1)}, u32[]{:S(2)}) copy-start(bf16[2048,16]{0,1:T(8,128)(2,1)} %param.23) | copy-start | bytes 196612
  6.5 3.8 copy-start.2
  6.5 9.1 %copy-start.1 = (bf16[2,256,128]{2,1,0:T(8,128)(2,1)S(1)}, bf16[2,256,128]{2,1,0:T(8,128)(2,1)}, u32[]{:S(2)}) copy-start(bf16[2,256,128]{2,1,0:T(8,128)(2,1)} %param.15) | copy-start | bytes 393220
  6.5 9.3 %copy-start.5 = (f32[128]{0:T(128)S(1)}, f32[128]{0:T(128)}, u32[]{:S(2)}) copy-start(f32[128]{0:T(128)} %param.19) | copy-start | bytes 1540
  6.5 64.2 %all-gather.5.cloned.1.call-start = ((), (), s32[]{:S(2)}) async-start(), calls=%async_computation.3 | async-start | bytes 6291456 | tf_op jit(solution)/shard_map/all_gather | solution.py:99
  7.3 23.3 %copy-start.6 = (f32[128]{0:T(128)S(1)}, f32[128]{0:T(128)}, u32[]{:S(2)}) copy-start(f32[128]{0:T(128)} %param.18) | copy-start | bytes 1540
  7.3 115.3 %reduce-scatter.2.cloned.1.call-start = ((), (), s32[]{:S(2)}) async-start(), calls=%async_computation.4 | async-start | bytes 5242880 | tf_op jit(solution)/shard_map/reduce_scatter | solution.py:110
  77.2 0.7 copy-start.4
  77.2 47.1 %copy-start.3 = (f32[2048]{0:T(1024)S(1)}, f32[2048]{0:T(1024)}, u32[]{:S(2)}) copy-start(f32[2048]{0:T(1024)} %param.22) | copy-start | bytes 24580
  133.8 110.5 %all-to-all-start = ((bf16[16,72,2048]{2,1,0:T(8,128)(2,1)}), bf16[16,72,2048]{2,1,0:T(8,128)(2,1)}, u32[]{:S(2)}, u32[]{:S(2)}) async-start(bf16[16,72,2048]{2,1,0:T(8,128)(2,1)} %bitcast.101), calls=%async_computation.1 | async-start | bytes 9437184 | tf_op jit(solution)/shard_map/all_to_all | solution.py:130
  138.6 48.7 %all-gather.7.cloned.1.call-start = ((), (), s32[]{:S(2)}) async-start(), calls=%async_computation.5 | async-start | bytes 4718592 | tf_op jit(solution)/shard_map/all_gather | solution.py:103
  139.3 114.3 %all-gather.9.cloned.1.call-start = ((), (), s32[]{:S(2)}) async-start(), calls=%async_computation.6 | async-start | bytes 4718592 | tf_op jit(solution)/shard_map/all_gather | solution.py:104
  139.9 140.2 %all-gather.11.cloned.1.call-start = ((), (), s32[]{:S(2)}) async-start(), calls=%async_computation.7 | async-start | bytes 4718592 | tf_op jit(solution)/shard_map/all_gather | solution.py:105
  287.6 111.3 %all-to-all-start.1 = ((bf16[16,72,2048]{2,1,0:T(8,128)(2,1)}), bf16[16,72,2048]{2,1,0:T(8,128)(2,1)}, u32[]{:S(2)}, u32[]{:S(2)}) async-start(bf16[16,72,2048]{2,1,0:T(8,128)(2,1)} %bitcast.102), calls=%async_computation.2 | async-start | bytes 9437184 | tf_op jit(solution)/shard_map/all_to_all | solution.py:135
Sparse Core Ops, SparseCore 0:
  8.9 61.7 all-gather.4
  77.4 45.2 reduce-scatter.1
  141.1 46.1 all-gather.6
  188.7 44.9 all-gather.8
  235.2 44.9 all-gather.10
where the time goes:
time: 425 us
  waiting for transfers between devices  304 us (72%)
  matrix products  35.9 us (8%)
  local copies, waits for them, and re-layouts  24.7 us (6%)
  blocking collectives  19.5 us (5%)
  other arithmetic  16.6 us (4%)
  between operations  13.4 us (3%)
  starting transfers between devices  10.6 us (2%)
    all_to_all x1, waiting for transfers between devices, shards(): lax.all_to_all(served, ('tp', 'ep'), split_axis=0, concat_axis=0, tiled=T...  105 us
    all_to_all x1, waiting for transfers between devices, shards(): lax.all_to_all(buffer, ('tp', 'ep'), split_axis=0, concat_axis=0, tiled=T...  57 us
    all_gather x1, waiting for transfers between devices, shards(): lax.all_gather(expert_gate, 'cp', axis=2, tiled=True)  46.8 us
    reduce_scatter x1, waiting for transfers between devices, shards(): lax.psum_scatter(partial_proj, 'tp', scatter_dimension=1, tiled=True)  39.1 us
    all_gather x1, waiting for transfers between devices, shards(): lax.all_gather(out_weight, 'cp', axis=1, tiled=True)  35.5 us
    all_gather x1, waiting for transfers between devices, shards(): lax.all_gather(expert_down, 'cp', axis=2, tiled=True)  18 us
    gather x1, local copies, waits for them, and re-layouts, shards(): back.reshape(experts * dev_cap, width)[target]  11.8 us
    dot_general x1, matrix products, expert_rows(): jnp.dot(flat_rows, full_gate[0], preferred_element_type=jnp.float32)  9.4 us
  transfers between devices with their start and end apart: 7, of which 6 were waited for; matrix products, arithmetic and copies ran while one was open for 8% of the time, Pallas kernels for 0%

commit v1 on v0

--- a/solution.py
+++ b/solution.py
@@ -62,6 +62,28 @@
     expert_up,
     expert_down,
 ):
+
+    def plan_the_skins(work_x, axis_k, which_dim):
+        heard = lax.axis_size(("tp", "ep"))
+        frame_out, d_next = (heard, lax.axis_index(("tp", "ep")))
+        earlier = work_x.shape[axis_k] // frame_out
+        ready = list(work_x.shape)
+        ready[axis_k] = earlier
+        r_now = ready[which_dim]
+        ready[which_dim] = r_now * frame_out
+        taken_in = jnp.zeros(ready, work_x.dtype)
+        for no in range(frame_out):
+            main = lax.dynamic_slice_in_dim(work_x, (d_next ^ no) * earlier, earlier, axis=axis_k)
+            if no:
+                in_order = []
+                for i in range(frame_out):
+                    in_order.append((i, i ^ no))
+                main = lax.ppermute(main, ("tp", "ep"), in_order)
+            taken_in = lax.dynamic_update_slice_in_dim(
+                taken_in, main, (d_next ^ no) * r_now, axis=which_dim
+            )
+        return taken_in
+
     packs = query.shape[0]
     row_count = query.shape[1]
     head_count = query.shape[2] // HEAD_WIDTH
@@ -126,12 +148,7 @@
         .set(sent_rows)
         .reshape(experts, dev_cap, width)
     )
-    served = expert_rows(
-        lax.all_to_all(buffer, ("tp", "ep"), split_axis=0, concat_axis=0, tiled=True),
-        full_gate,
-        full_up,
-        full_down,
-    )
+    served = expert_rows(plan_the_skins(buffer, 0, 0), full_gate, full_up, full_down)
     back = lax.all_to_all(served, ("tp", "ep"), split_axis=0, concat_axis=0, tiled=True)
     picked = back.reshape(experts * dev_cap, width)[target].reshape(packs * share, top_count, width)
     mixture = jnp.sum(gates[:, :, None] * picked.astype(jnp.float32), axis=1)

time: 425 us -> 411 us (0.967)
  waiting for transfers between devices: 304 us -> 228 us
  starting transfers between devices: 10.6 us -> 54.6 us
  local copies, waits for them, and re-layouts: 24.7 us -> 43.3 us
    all_to_all x1 -> x0, waiting for transfers between devices: 57 us -> none  [shards(): lax.all_to_all(buffer, ('tp', 'ep'), split_axis=0, concat_axis=0, tiled=T...]
    all_gather x1, waiting for transfers between devices: 46.8 us -> 0.01 us  [shards(): lax.all_gather(expert_gate, 'cp', axis=2, tiled=True)]
    ppermute x0 -> x15, waiting for transfers between devices: none -> 45.3 us  [plan_the_skins(): main = lax.ppermute(main, ('tp', 'ep'), in_order)]
    ppermute x0 -> x15, starting transfers between devices: none -> 44.7 us  [plan_the_skins(): main = lax.ppermute(main, ('tp', 'ep'), in_order)]
    all_gather x1, waiting for transfers between devices: 18 us -> 1.5 us  [shards(): lax.all_gather(expert_down, 'cp', axis=2, tiled=True)]
    dynamic_update_slice x0 -> x15, local copies, waits for them, and re-layouts: none -> 13 us  [plan_the_skins(): lax.dynamic_update_slice_in_dim(taken_in, main, (d_next ^ no) * r_now, ax...]
    all_to_all x1 -> x0, starting transfers between devices: 4.77 us -> none  [shards(): lax.all_to_all(buffer, ('tp', 'ep'), split_axis=0, concat_axis=0, tiled=T...]
  transfers between devices with their start and end apart: 7 -> 21, of which waited for: 6 -> 10; matrix products, arithmetic and copies ran while one was open for 8% -> 14% of each run, Pallas kernels for 0% -> 0%
where the time goes in v1:
time: 411 us
  waiting for transfers between devices  228 us (55%)
  starting transfers between devices  54.6 us (13%)
  local copies, waits for them, and re-layouts  43.3 us (11%)
  matrix products  35.5 us (9%)
  blocking collectives  19.4 us (5%)
  other arithmetic  16.6 us (4%)
  between operations  13.6 us (3%)
    all_to_all x1, waiting for transfers between devices, shards(): lax.all_to_all(served, ('tp', 'ep'), split_axis=0, concat_axis=0, tiled=T...  105 us
    ppermute x15, waiting for transfers between devices, plan_the_skins(): main = lax.ppermute(main, ('tp', 'ep'), in_order)  45.3 us
    ppermute x15, starting transfers between devices, plan_the_skins(): main = lax.ppermute(main, ('tp', 'ep'), in_order)  44.7 us
    reduce_scatter x1, waiting for transfers between devices, shards(): lax.psum_scatter(partial_proj, 'tp', scatter_dimension=1, tiled=True)  38.4 us
    all_gather x1, waiting for transfers between devices, shards(): lax.all_gather(out_weight, 'cp', axis=1, tiled=True)  35.6 us
    dynamic_update_slice x15, local copies, waits for them, and re-layouts, plan_the_skins(): lax.dynamic_update_slice_in_dim(taken_in, main, (d_next ^ no) * r_now, ax...  13 us
    gather x1, local copies, waits for them, and re-layouts, shards(): back.reshape(experts * dev_cap, width)[target]  11.8 us
    all_to_all x1, starting transfers between devices, shards(): lax.all_to_all(served, ('tp', 'ep'), split_axis=0, concat_axis=0, tiled=T...  9.78 us
  transfers between devices with their start and end apart: 21, of which 10 were waited for; matrix products, arithmetic and copies ran while one was open for 14% of the time, Pallas kernels for 0%

profile of v1, /device:TPU:0, one launch (start us, length us, event | category | flops | bytes accessed | tf_op | source)
XLA Modules:
  0.0 410.9 jit_solution(6522443817320301052)
XLA Ops:
  10.5 5.2 %all_gather.21 = bf16[2,512]{1,0:T(2,128)(2,1)S(1)} all-gather(bf16[2,256]{1,0:T(2,128)(2,1)S(1)} %convert_element_type.52), channel_id=1, replica_groups=mesh['cp'=2,'tp'=4,'ep'=4] {'cp'}, dimensions={1}, use_global_device_ids=true | all-gather | bytes 3072 | tf_op jit(solution)/shard_map/all_gather | solution.py:101
  16.0 5.7 %all_gather.22 = bf16[2,512,128]{2,1,0:T(8,128)(2,1)S(1)} all-gather(bf16[2,256,128]{2,1,0:T(8,128)(2,1)S(1)} %fusion.33), channel_id=1, replica_groups=mesh['cp'=2,'tp'=4,'ep'=4] {'cp'}, dimensions={1}, use_global_device_ids=true | all-gather | bytes 393216 | tf_op jit(solution)/shard_map/all_gather | solution.py:99
  21.6 8.5 %all_gather.23 = bf16[2,512,128]{1,2,0:T(8,128)(2,1)S(1)} all-gather(bf16[2,256,128]{1,2,0:T(8,128)(2,1)S(1)} %copy.60), channel_id=1, replica_groups=mesh['cp'=2,'tp'=4,'ep'=4] {'cp'}, dimensions={1}, use_global_device_ids=true | all-gather | bytes 393216 | tf_op jit(solution)/shard_map/all_gather | solution.py:100
  35.1 35.6 %all-gather.5.cloned.1.call-done = bf16[1024,2048]{1,0:T(8,128)(2,1)} async-done(((bf16[1024,1024]{1,0:T(8,128)(2,1)}), bf16[1024,2048]{1,0:T(8,128)(2,1)}) %all-gather.5.cloned.1.call-update) | async-done | bytes 4194320 | tf_op jit(solution)/shard_map/all_gather | solution.py:121
  70.7 6.5 %fusion.7 = f32[2,256,2048]{2,1,0:T(8,128)} fusion(bf16[2,256,1024]{1,2,0:T(8,128)(2,1)S(1)} %bitcast.108, bf16[1024,2048]{1,0:T(8,128)(2,1)} %all-gather.5.cloned.1.call-done), kind=kOutput, calls=%fused_computation.11 | convolution fusion | flops 2147483648 | bytes 9437184 | tf_op jit(solution)/shard_map/dot_general | solution.py:119
  79.1 4.5 %reduce-window.6 = s32[16,8,128]{2,1,0:T(8,128)S(1)} reduce-window(s32[16,8,128]{2,1,0:T(8,128)S(1)} %fusion.39, s32[]{:T(128)} %constant.30.clone.1), window={size=1x1x128 pad=0_0x0_0x127_0}, to_apply=%region_7.8 | reduce-window | flops 2080768 | bytes 131076 | tf_op jit(solution)/shard_map/reduce-window
  84.4 38.4 %reduce-scatter.2.cloned.1.call-done = f32[2,64,2048]{2,1,0:T(8,128)} async-done(((f32[2,256,2048]{2,1,0:T(8,128)}), f32[2,64,2048]{2,1,0:T(8,128)}) %reduce-scatter.2.cloned.1.call-update) | async-done | bytes 1048592 | tf_op jit(solution)/shard_map/reduce_scatter | solution.py:132
  124.6 9.3 %scatter_custom_fusion = bf16[1152,2048]{1,0:T(8,128)(2,1)} fusion(s32[1024]{0:T(1024)S(1)} %bitcast.113, bf16[]{:T(256)} %constant.14.clone.1, bf16[128,2048]{1,0:T(8,128)(2,1)S(1)} %fusion.28), kind=kCustom, calls=%fused_computation.9 | custom fusion | bytes 5242882 | tf_op jit(solution)/shard_map/scatter | solution.py:148
  141.8 2.4 collective-permute-start.1
  145.5 10.5 %collective-permute-done = bf16[1,72,2048]{2,1,0:T(8,128)(2,1)} collective-permute-done((bf16[1,72,2048]{2,1,0:T(8,128)(2,1)}, bf16[1,72,2048]{2,1,0:T(8,128)(2,1)}, u32[]{:S(2)}, u32[]{:S(2)}) %collective-permute-start) | collective-permute-done | bytes 294944 | tf_op jit(solution)/shard_map/ppermute | solution.py:81
  157.7 8.0 %collective-permute-done.1 = bf16[1,72,2048]{2,1,0:T(8,128)(2,1)} collective-permute-done((bf16[1,72,2048]{2,1,0:T(8,128)(2,1)}, bf16[1,72,2048]{2,1,0:T(8,128)(2,1)}, u32[]{:S(2)}, u32[]{:S(2)}) %collective-permute-start.1) | collective-permute-done | bytes 294944 | tf_op jit(solution)/shard_map/ppermute | solution.py:81
  168.7 18.6 %collective-permute-start.8 = (bf16[1,72,2048]{2,1,0:T(8,128)(2,1)}, bf16[1,72,2048]{2,1,0:T(8,128)(2,1)S(1)}, u32[]{:S(2)}, u32[]{:S(2)}) collective-permute-start(bf16[1,72,2048]{2,1,0:T(8,128)(2,1)} %get-tuple-element.15), channel_id=1, source_target_pairs={{0,9},{1,8},{2,11},{3,10},{4,13},{5,12},{6,15},{7,14},{8,1},{9,0},... | collective-permute-start | bytes 884744 | tf_op jit(solution)/shard_map/ppermute | solution.py:81
  194.5 10.0 %collective-permute-start.11 = (bf16[1,72,2048]{2,1,0:T(8,128)(2,1)S(1)}, bf16[1,72,2048]{2,1,0:T(8,128)(2,1)S(1)}, u32[]{:S(2)}, u32[]{:S(2)}) collective-permute-start(bf16[1,72,2048]{2,1,0:T(8,128)(2,1)S(1)} %get-tuple-element.12), channel_id=1, source_target_pairs={{0,12},{1,13},{2,14},{3,15},{4,8},{5,9},{6,10},{7,11},{8,4},{9,5},... | collective-permute-start | bytes 884744 | tf_op jit(solution)/shard_map/ppermute | solution.py:81
  205.2 6.3 %collective-permute-start.12 = (bf16[1,72,2048]{2,1,0:T(8,128)(2,1)S(1)}, bf16[1,72,2048]{2,1,0:T(8,128)(2,1)S(1)}, u32[]{:S(2)}, u32[]{:S(2)}) collective-permute-start(bf16[1,72,2048]{2,1,0:T(8,128)(2,1)S(1)} %get-tuple-element.11), channel_id=1, source_target_pairs={{0,13},{1,12},{2,15},{3,14},{4,9},{5,8},{6,11},{7,10},{8,5},{9,4},... | collective-permute-start | bytes 884744 | tf_op jit(solution)/shard_map/ppermute | solution.py:81
  213.5 2.8 collective-permute-done.9
  217.9 5.8 %collective-permute-done.11 = bf16[1,72,2048]{2,1,0:T(8,128)(2,1)S(1)} collective-permute-done((bf16[1,72,2048]{2,1,0:T(8,128)(2,1)S(1)}, bf16[1,72,2048]{2,1,0:T(8,128)(2,1)S(1)}, u32[]{:S(2)}, u32[]{:S(2)}) %collective-permute-start.11) | collective-permute-done | bytes 294944 | tf_op jit(solution)/shard_map/ppermute | solution.py:81
  225.1 16.7 %collective-permute-done.13 = bf16[1,72,2048]{2,1,0:T(8,128)(2,1)S(1)} collective-permute-done((bf16[1,72,2048]{2,1,0:T(8,128)(2,1)S(1)}, bf16[1,72,2048]{2,1,0:T(8,128)(2,1)S(1)}, u32[]{:S(2)}, u32[]{:S(2)}) %collective-permute-start.13) | collective-permute-done | bytes 294944 | tf_op jit(solution)/shard_map/ppermute | solution.py:81
  243.3 8.9 %fusion.17 = f32[1152,768]{1,0:T(8,128)} fusion(bf16[1152,2048]{1,0:T(8,128)(2,1)} %bitcast.105, bf16[1,2048,768]{2,1,0:T(8,128)(2,1)} %all-gather.7.cloned.1.call-done), kind=kOutput, calls=%fused_computation.20 | convolution fusion | flops 3623878656 | bytes 11403264 | tf_op jit(solution)/shard_map/dot_general | solution.py:40
  252.2 8.5 %multiply_convert_fusion = bf16[1152,768]{1,0:T(8,128)(2,1)S(1)} fusion(f32[1152,768]{1,0:T(8,128)} %fusion.17, bf16[1152,2048]{1,0:T(8,128)(2,1)} %bitcast.106, bf16[1,2048,768]{2,1,0:T(8,128)(2,1)} %all-gather.9.cloned.1.call-done), kind=kOutput, calls=%fused_computation.16 | convolution fusion | flops 3629187072 | bytes 13172736 | tf_op jit(solution)/shard_map/dot_general | solution.py:41
  262.2 7.4 %convolution_convert_fusion = bf16[1152,2048]{1,0:T(8,128)(2,1)} fusion(bf16[1152,768]{1,0:T(8,128)(2,1)S(1)} %multiply_convert_fusion, bf16[1,2048,768]{2,1,0:T(8,128)(2,1)} %all-gather.11.cloned.1.call-done), kind=kOutput, calls=%fused_computation.5 | convolution fusion | flops 3626237952 | bytes 9633792 | tf_op jit(solution)/shard_map/rf,df->rd/dot_general | solution.py:43
  269.7 9.8 %all-to-all-start = ((bf16[16,72,2048]{2,1,0:T(8,128)(2,1)}), bf16[16,72,2048]{2,1,0:T(8,128)(2,1)}, u32[]{:S(2)}, u32[]{:S(2)}) async-start(bf16[16,72,2048]{2,1,0:T(8,128)(2,1)} %bitcast.104), calls=%async_computation.1 | async-start | bytes 9437184 | tf_op jit(solution)/shard_map/all_to_all | solution.py:152
  280.0 105.2 %all-to-all-done = bf16[16,72,2048]{2,1,0:T(8,128)(2,1)} async-done(((bf16[16,72,2048]{2,1,0:T(8,128)(2,1)}), bf16[16,72,2048]{2,1,0:T(8,128)(2,1)}, u32[]{:S(2)}, u32[]{:S(2)}) %all-to-all-start) | async-done | bytes 4718624 | tf_op jit(solution)/shard_map/all_to_all | solution.py:152
  385.1 11.8 %gather_fusion = bf16[1024,2048]{1,0:T(8,128)(2,1)} fusion(bf16[1152,2048]{1,0:T(8,128)(2,1)} %bitcast.21, s32[1024]{0:T(1024)S(1)} %broadcast_clamp_fusion), kind=kCustom, calls=%fused_computation | custom fusion | bytes 8392704 | tf_op jit(solution)/shard_map/gather | solution.py:153
  396.9 6.5 %fusion = f32[128,2048]{1,0:T(8,128)S(1)} fusion(bf16[1024,2048]{1,0:T(8,128)(2,1)} %gather_fusion, f32[128,8]{1,0:T(8,128)S(1)} %copy.64), kind=kLoop, calls=%fused_computation.3 | loop fusion | flops 6029312 | bytes 5246976 | tf_op jit(solution)/shard_map/reduce_sum | solution.py:154
  (111 shorter events, 44.4 us)
Async XLA Ops:
  6.5 273.0 %copy-start = (bf16[2048,16]{0,1:T(8,128)(2,1)S(1)}, bf16[2048,16]{0,1:T(8,128)(2,1)}, u32[]{:S(2)}) copy-start(bf16[2048,16]{0,1:T(8,128)(2,1)} %param.23) | copy-start | bytes 196612
  6.5 23.9 %copy-start.8 = (f32[128]{0:T(128)S(1)}, f32[128]{0:T(128)}, u32[]{:S(2)}) copy-start(f32[128]{0:T(128)} %param.18) | copy-start | bytes 1540
  6.5 64.2 %all-gather.5.cloned.1.call-start = ((), (), s32[]{:S(2)}) async-start(), calls=%async_computation.2 | async-start | bytes 6291456 | tf_op jit(solution)/shard_map/all_gather | solution.py:121
  7.3 115.5 %reduce-scatter.2.cloned.1.call-start = ((), (), s32[]{:S(2)}) async-start(), calls=%async_computation.3 | async-start | bytes 5242880 | tf_op jit(solution)/shard_map/reduce_scatter | solution.py:132
  77.2 47.2 %copy-start.5 = (f32[2048]{0:T(1024)S(1)}, f32[2048]{0:T(1024)}, u32[]{:S(2)}) copy-start(f32[2048]{0:T(1024)} %param.22) | copy-start | bytes 24580
  77.3 166.0 %all-gather.7.cloned.1.call-start = ((), (), s32[]{:S(2)}) async-start(), calls=%async_computation.4 | async-start | bytes 4718592 | tf_op jit(solution)/shard_map/all_gather | solution.py:125
  78.0 174.2 %all-gather.9.cloned.1.call-start = ((), (), s32[]{:S(2)}) async-start(), calls=%async_computation.5 | async-start | bytes 4718592 | tf_op jit(solution)/shard_map/all_gather | solution.py:126
  78.6 183.7 %all-gather.11.cloned.1.call-start = ((), (), s32[]{:S(2)}) async-start(), calls=%async_computation.6 | async-start | bytes 4718592 | tf_op jit(solution)/shard_map/all_gather | solution.py:127
  140.3 15.7 %collective-permute-start = (bf16[1,72,2048]{2,1,0:T(8,128)(2,1)}, bf16[1,72,2048]{2,1,0:T(8,128)(2,1)}, u32[]{:S(2)}, u32[]{:S(2)}) collective-permute-start(bf16[1,72,2048]{2,1,0:T(8,128)(2,1)} %get-tuple-element.23), channel_id=1, source_target_pairs={{0,1},{1,0},{2,3},{3,2},{4,5},{5,4},{6,7},{7,6},{8,9},{9,8},{10,11... | collective-permute-start | bytes 884744 | tf_op jit(solution)/shard_map/ppermute | solution.py:81
  141.8 23.8 %collective-permute-start.1 = (bf16[1,72,2048]{2,1,0:T(8,128)(2,1)}, bf16[1,72,2048]{2,1,0:T(8,128)(2,1)}, u32[]{:S(2)}, u32[]{:S(2)}) collective-permute-start(bf16[1,72,2048]{2,1,0:T(8,128)(2,1)} %get-tuple-element.22), channel_id=1, source_target_pairs={{0,2},{1,3},{2,0},{3,1},{4,6},{5,7},{6,4},{7,5},{8,10},{9,11},{10,... | collective-permute-start | bytes 884744 | tf_op jit(solution)/shard_map/ppermute | solution.py:81
  144.3 23.1 %collective-permute-start.2 = (bf16[1,72,2048]{2,1,0:T(8,128)(2,1)}, bf16[1,72,2048]{2,1,0:T(8,128)(2,1)S(1)}, u32[]{:S(2)}, u32[]{:S(2)}) collective-permute-start(bf16[1,72,2048]{2,1,0:T(8,128)(2,1)} %get-tuple-element.21), channel_id=1, source_target_pairs={{0,3},{1,2},{2,1},{3,0},{4,7},{5,6},{6,5},{7,4},{8,11},{9,10},{10,... | collective-permute-start | bytes 884744 | tf_op jit(solution)/shard_map/ppermute | solution.py:81
  144.8 24.0 %collective-permute-start.3 = (bf16[1,72,2048]{2,1,0:T(8,128)(2,1)}, bf16[1,72,2048]{2,1,0:T(8,128)(2,1)S(1)}, u32[]{:S(2)}, u32[]{:S(2)}) collective-permute-start(bf16[1,72,2048]{2,1,0:T(8,128)(2,1)} %get-tuple-element.20), channel_id=1, source_target_pairs={{0,4},{1,5},{2,6},{3,7},{4,0},{5,1},{6,2},{7,3},{8,12},{9,13},{10,... | collective-permute-start | bytes 884744 | tf_op jit(solution)/shard_map/ppermute | solution.py:81
  144.8 43.3 %collective-permute-start.4 = (bf16[1,72,2048]{2,1,0:T(8,128)(2,1)}, bf16[1,72,2048]{2,1,0:T(8,128)(2,1)S(1)}, u32[]{:S(2)}, u32[]{:S(2)}) collective-permute-start(bf16[1,72,2048]{2,1,0:T(8,128)(2,1)} %get-tuple-element.19), channel_id=1, source_target_pairs={{0,5},{1,4},{2,7},{3,6},{4,1},{5,0},{6,3},{7,2},{8,13},{9,12},{10,... | collective-permute-start | bytes 884744 | tf_op jit(solution)/shard_map/ppermute | solution.py:81
  156.0 35.3 %collective-permute-start.5 = (bf16[1,72,2048]{2,1,0:T(8,128)(2,1)}, bf16[1,72,2048]{2,1,0:T(8,128)(2,1)S(1)}, u32[]{:S(2)}, u32[]{:S(2)}) collective-permute-start(bf16[1,72,2048]{2,1,0:T(8,128)(2,1)} %get-tuple-element.18), channel_id=1, source_target_pairs={{0,6},{1,7},{2,4},{3,5},{4,2},{5,3},{6,0},{7,1},{8,14},{9,15},{10,... | collective-permute-start | bytes 884744 | tf_op jit(solution)/shard_map/ppermute | solution.py:81
  165.7 28.8 %collective-permute-start.6 = (bf16[1,72,2048]{2,1,0:T(8,128)(2,1)}, bf16[1,72,2048]{2,1,0:T(8,128)(2,1)S(1)}, u32[]{:S(2)}, u32[]{:S(2)}) collective-permute-start(bf16[1,72,2048]{2,1,0:T(8,128)(2,1)} %get-tuple-element.17), channel_id=1, source_target_pairs={{0,7},{1,6},{2,5},{3,4},{4,3},{5,2},{6,1},{7,0},{8,15},{9,14},{10,... | collective-permute-start | bytes 884744 | tf_op jit(solution)/shard_map/ppermute | solution.py:81
  167.4 37.8 %collective-permute-start.7 = (bf16[1,72,2048]{2,1,0:T(8,128)(2,1)}, bf16[1,72,2048]{2,1,0:T(8,128)(2,1)S(1)}, u32[]{:S(2)}, u32[]{:S(2)}) collective-permute-start(bf16[1,72,2048]{2,1,0:T(8,128)(2,1)} %get-tuple-element.16), channel_id=1, source_target_pairs={{0,8},{1,9},{2,10},{3,11},{4,12},{5,13},{6,14},{7,15},{8,0},{9,1},... | collective-permute-start | bytes 884744 | tf_op jit(solution)/shard_map/ppermute | solution.py:81
  168.7 43.5 %collective-permute-start.8 = (bf16[1,72,2048]{2,1,0:T(8,128)(2,1)}, bf16[1,72,2048]{2,1,0:T(8,128)(2,1)S(1)}, u32[]{:S(2)}, u32[]{:S(2)}) collective-permute-start(bf16[1,72,2048]{2,1,0:T(8,128)(2,1)} %get-tuple-element.15), channel_id=1, source_target_pairs={{0,9},{1,8},{2,11},{3,10},{4,13},{5,12},{6,15},{7,14},{8,1},{9,0},... | collective-permute-start | bytes 884744 | tf_op jit(solution)/shard_map/ppermute | solution.py:81
  188.1 28.2 %collective-permute-start.9 = (bf16[1,72,2048]{2,1,0:T(8,128)(2,1)S(1)}, bf16[1,72,2048]{2,1,0:T(8,128)(2,1)S(1)}, u32[]{:S(2)}, u32[]{:S(2)}) collective-permute-start(bf16[1,72,2048]{2,1,0:T(8,128)(2,1)S(1)} %get-tuple-element.14), channel_id=1, source_target_pairs={{0,10},{1,11},{2,8},{3,9},{4,14},{5,15},{6,12},{7,13},{8,2},{9,3},... | collective-permute-start | bytes 884744 | tf_op jit(solution)/shard_map/ppermute | solution.py:81
  191.3 25.8 %collective-permute-start.10 = (bf16[1,72,2048]{2,1,0:T(8,128)(2,1)S(1)}, bf16[1,72,2048]{2,1,0:T(8,128)(2,1)S(1)}, u32[]{:S(2)}, u32[]{:S(2)}) collective-permute-start(bf16[1,72,2048]{2,1,0:T(8,128)(2,1)S(1)} %get-tuple-element.13), channel_id=1, source_target_pairs={{0,11},{1,10},{2,9},{3,8},{4,15},{5,14},{6,13},{7,12},{8,3},{9,2},... | collective-permute-start | bytes 884744 | tf_op jit(solution)/shard_map/ppermute | solution.py:81
  194.5 29.2 %collective-permute-start.11 = (bf16[1,72,2048]{2,1,0:T(8,128)(2,1)S(1)}, bf16[1,72,2048]{2,1,0:T(8,128)(2,1)S(1)}, u32[]{:S(2)}, u32[]{:S(2)}) collective-permute-start(bf16[1,72,2048]{2,1,0:T(8,128)(2,1)S(1)} %get-tuple-element.12), channel_id=1, source_target_pairs={{0,12},{1,13},{2,14},{3,15},{4,8},{5,9},{6,10},{7,11},{8,4},{9,5},... | collective-permute-start | bytes 884744 | tf_op jit(solution)/shard_map/ppermute | solution.py:81
  205.2 19.2 %collective-permute-start.12 = (bf16[1,72,2048]{2,1,0:T(8,128)(2,1)S(1)}, bf16[1,72,2048]{2,1,0:T(8,128)(2,1)S(1)}, u32[]{:S(2)}, u32[]{:S(2)}) collective-permute-start(bf16[1,72,2048]{2,1,0:T(8,128)(2,1)S(1)} %get-tuple-element.11), channel_id=1, source_target_pairs={{0,13},{1,12},{2,15},{3,14},{4,9},{5,8},{6,11},{7,10},{8,5},{9,4},... | collective-permute-start | bytes 884744 | tf_op jit(solution)/shard_map/ppermute | solution.py:81
  212.3 29.6 %collective-permute-start.13 = (bf16[1,72,2048]{2,1,0:T(8,128)(2,1)S(1)}, bf16[1,72,2048]{2,1,0:T(8,128)(2,1)S(1)}, u32[]{:S(2)}, u32[]{:S(2)}) collective-permute-start(bf16[1,72,2048]{2,1,0:T(8,128)(2,1)S(1)} %get-tuple-element.10), channel_id=1, source_target_pairs={{0,14},{1,15},{2,12},{3,13},{4,10},{5,11},{6,8},{7,9},{8,6},{9,7},... | collective-permute-start | bytes 884744 | tf_op jit(solution)/shard_map/ppermute | solution.py:81
  216.3 26.2 %collective-permute-start.14 = (bf16[1,72,2048]{2,1,0:T(8,128)(2,1)S(1)}, bf16[1,72,2048]{2,1,0:T(8,128)(2,1)S(1)}, u32[]{:S(2)}, u32[]{:S(2)}) collective-permute-start(bf16[1,72,2048]{2,1,0:T(8,128)(2,1)S(1)} %get-tuple-element.9), channel_id=1, source_target_pairs={{0,15},{1,14},{2,13},{3,12},{4,11},{5,10},{6,9},{7,8},{8,7},{9,6},... | collective-permute-start | bytes 884744 | tf_op jit(solution)/shard_map/ppermute | solution.py:81
  269.7 115.5 %all-to-all-start = ((bf16[16,72,2048]{2,1,0:T(8,128)(2,1)}), bf16[16,72,2048]{2,1,0:T(8,128)(2,1)}, u32[]{:S(2)}, u32[]{:S(2)}) async-start(bf16[16,72,2048]{2,1,0:T(8,128)(2,1)} %bitcast.104), calls=%async_computation.1 | async-start | bytes 9437184 | tf_op jit(solution)/shard_map/all_to_all | solution.py:152
  (6 other events, 28.5 us)
Sparse Core Ops, SparseCore 0:
  8.9 61.7 all-gather.4
  77.4 45.3 reduce-scatter.1
  124.4 44.9 all-gather.6
  170.8 44.9 all-gather.8
  217.3 44.9 all-gather.10
